TPU v7x, 128 devices: a whole 4x4x4 slice. The times are simulated.
128 devices in a mesh: rows: 32 (over y, x, z_lo), cols: 4 (over z_hi, core).
Axes of the slice: x: 4, y: 4, z: 4 (z_hi: 2, z_lo: 2; z = z_hi * 2 + z_lo), core: 2. Of those that a mesh axis runs over, the one named last changes fastest.
Arguments:
- block_input: bfloat16 [2, 128, 128, 1536], P(None, 'rows', 'cols'), may hold values from -6 to 6
- token_grads: bfloat16 [2, 4096, 6144], P(None, ('rows', 'cols')), may hold values from -6 to 6
- conv_kernel: float32 [7, 7, 1536], replicated, may hold values from -0.875 to 0.875
- layer_norm_gain: float32 [1536], replicated, may hold values from 0.25 to 1.75
- w_in: bfloat16 [1536, 3072], P('rows', 'cols'), may hold values from -0.15625 to 0.15625
- w_out: bfloat16 [3072, 1536], P('cols', 'rows'), may hold values from -0.109375 to 0.109375
- layer_scale: float32 [1536], replicated, may hold values from 0.25 to 1.75
Outputs:
- input_grad: bfloat16 [2, 128, 128, 1536], P(None, 'rows', 'cols')
- grad_w1: float32 [1536, 3072], P('rows', 'cols')
- grad_w2: float32 [3072, 1536], P('cols', 'rows')
- grad_kernel: float32 [7, 7, 1536], replicated
All inputs are finite; a program needn't handle non-finite values.
Results may differ from a plain program's by a relative error of at most 0.0062.
Values may be sent and summed in bfloat16 or wider, within the bound.
No kernel may reach another device: no remote copies, remote signals or barrier semaphores. Data moves between devices by JAX's collectives and lax.ppermute only.
A program may use at most 128 MiB of HBM per device.

v0:
```python
import jax
import jax.numpy as jnp
from jax import lax
from jax.sharding import PartitionSpec as P


def with_halo(value, sides, width):
    for axis, dim in sides:
        peers, length = (lax.axis_size(axis), value.shape[dim])
        up = [(i, (i + 1) % peers) for i in range(peers - 1)]
        down = [(j, i) for i, j in up]
        last = lax.slice_in_dim(value, length - width, length, axis=dim)
        first = lax.slice_in_dim(value, 0, width, axis=dim)
        before = lax.ppermute(last, axis, up)
        after = lax.ppermute(first, axis, down)
        value = jnp.concatenate([before, value, after], axis=dim)
    return value


def swap_with(value, axis, bit):
    peers = lax.axis_size(axis)
    return lax.ppermute(value, axis, [(i, i ^ (1 << bit)) for i in range(peers)])


def gather_rows(value, axis, order):
    me = lax.axis_index(axis)
    for bit in order:
        other = swap_with(value, axis, bit)
        b = (me >> bit) & 1
        both = jnp.concatenate([value, other, value], axis=0)
        value = lax.dynamic_slice_in_dim(both, b * value.shape[0], 2 * value.shape[0], axis=0)
    n = len(order)
    block = value.shape[0] >> n
    rest = value.shape[1:]
    value = value.reshape((2,) * n + (block,) + rest)
    perm = [n - 1 - order.index(k) for k in reversed(range(n))]
    value = value.transpose(perm + list(range(n, value.ndim)))
    return value.reshape((block << n,) + rest)


def scatter_rows(value, axis, order):
    me = lax.axis_index(axis)
    n = len(order)
    block = value.shape[0] >> n
    rest = value.shape[1:]
    value = value.reshape((2,) * n + (block,) + rest)
    perm = [n - 1 - order[j] for j in range(n)]
    value = value.transpose(perm + list(range(n, value.ndim))).reshape((block << n,) + rest)
    for bit in order:
        half = value.shape[0] // 2
        b = (me >> bit) & 1
        keep = lax.dynamic_slice_in_dim(value, b * half, half, axis=0)
        send = lax.dynamic_slice_in_dim(value, (1 - b) * half, half, axis=0)
        value = keep + swap_with(send, axis, bit)
    return value


GATHER_ORDERS = ((4, 2, 3, 1, 0), (2, 4, 0, 3, 1), (4, 2, 1, 0, 3))
SCATTER_ORDERS = ((0, 1, 3, 2, 4), (1, 3, 0, 4, 2), (3, 0, 1, 2, 4))


def scatter_split(value):
    third = value.shape[1] // 3
    return jnp.concatenate(
        [
            scatter_rows(value[:, i * third : (i + 1) * third], "rows", order)
            for i, order in enumerate(SCATTER_ORDERS)
        ],
        axis=1,
    )


def local(block_input, token_grads, conv_kernel, layer_norm_gain, w_in, w_out, layer_scale):
    images, tile_rows, tile_cols, channel_total = block_input.shape
    kernel_size = conv_kernel.shape[0]
    kernel_reach = kernel_size // 2
    n_rows = lax.axis_size("rows")
    n_cols = lax.axis_size("cols")
    row_bits = n_rows.bit_length() - 1
    col_bits = n_cols.bit_length() - 1
    run_count = tile_rows // 2
    half_cols = tile_cols // 2
    col_index = lax.axis_index("cols")

    hidden_cols = w_in.shape[1]
    both_weights = jnp.concatenate([w_in, w_out.T], axis=1)
    third = both_weights.shape[1] // 3
    gathered = jnp.concatenate(
        [
            gather_rows(both_weights[:, i * third : (i + 1) * third], "rows", order)
            for i, order in enumerate(GATHER_ORDERS)
        ],
        axis=1,
    )
    w_in_cols = gathered[:, :hidden_cols]
    w_out_cols_t = gathered[:, hidden_cols:]

    tokens = token_grads.reshape(images, 2, half_cols, 4 * channel_total)
    first_half = col_index // 2
    send_a = lax.dynamic_index_in_dim(tokens, first_half, 1, keepdims=False)
    send_b = lax.dynamic_index_in_dim(tokens, 1 - first_half, 1, keepdims=False)
    got_a = lax.ppermute(send_a, "cols", [(s, 2 * (s % 2) + s // 2) for s in range(n_cols)])
    got_b = lax.ppermute(send_b, "cols", [(s, 2 * (s % 2) + 1 - s // 2) for s in range(n_cols)])
    merged = lax.dynamic_slice_in_dim(
        jnp.stack([got_a, got_b, got_a], axis=1), col_index % 2, 2, axis=1
    )
    out_grad = merged.reshape(images, run_count, half_cols, 2, 2, channel_total)
    out_grad = out_grad.transpose(0, 1, 3, 2, 4, 5).reshape(
        images, tile_rows, tile_cols, channel_total
    )
    pixel_total = images * tile_rows * tile_cols
    branch_grad = (
        (out_grad.astype(jnp.float32) * layer_scale)
        .astype(jnp.bfloat16)
        .reshape(pixel_total, channel_total)
    )
    branch_all = lax.all_gather(branch_grad, "cols", axis=0, tiled=True)
    lane = 128
    groups = channel_total // lane

    def to_tiles(x):
        x = x.reshape(images, tile_rows, tile_cols, groups, lane).transpose(1, 2, 0, 3, 4)
        return x.reshape(tile_rows, tile_cols, images * groups, lane)

    def from_tiles(t):
        t = t.reshape(tile_rows, tile_cols, images, groups, lane).transpose(2, 0, 1, 3, 4)
        return t.reshape(images, tile_rows, tile_cols, channel_total)

    taps = jnp.tile(
        conv_kernel.reshape(kernel_size, kernel_size, 1, groups, lane), (1, 1, images, 1, 1)
    ).reshape(kernel_size, kernel_size, images * groups, lane)
    padded = with_halo(to_tiles(block_input), (("rows", 0), ("cols", 1)), kernel_reach)
    w_in_cols, w_out_cols_t, padded = lax.optimization_barrier((w_in_cols, w_out_cols_t, padded))
    conv_t = jnp.zeros((tile_rows, tile_cols, images * groups, lane), jnp.float32)
    for r in range(kernel_size):
        for s in range(kernel_size):
            conv_t = conv_t + taps[r, s] * padded[r : r + tile_rows, s : s + tile_cols].astype(
                jnp.float32
            )
    conv_out = from_tiles(conv_t)
    mean_val = jnp.mean(conv_out, axis=-1, keepdims=True)
    centered_input = conv_out - mean_val
    var_val = jnp.mean(centered_input * centered_input, axis=-1, keepdims=True)
    inverse_deviation = lax.rsqrt(var_val + 1e-06)
    standardized_input = centered_input * inverse_deviation
    norm_output = (
        (standardized_input * layer_norm_gain)
        .astype(jnp.bfloat16)
        .reshape(pixel_total, channel_total)
    )
    normed_all = lax.all_gather(norm_output, "cols", axis=0, tiled=True)
    pre = jnp.dot(normed_all, w_in_cols, preferred_element_type=jnp.float32)
    cdf = 0.5 * (1.0 + lax.erf(pre * 0.7071067811865476))
    hidden = (pre * cdf).astype(jnp.bfloat16)
    back_hidden = jnp.dot(branch_all, w_out_cols_t, preferred_element_type=jnp.float32)
    density = jnp.exp(-0.5 * pre * pre) * 0.3989422804014327
    hidden_grad = (back_hidden * (cdf + pre * density)).astype(jnp.bfloat16)
    scale = 1.0 / float(images * tile_rows * tile_cols * n_rows * n_cols) ** 0.5
    out_terms_t = lax.dot_general(
        branch_all, hidden, (((0,), (0,)), ((), ())), preferred_element_type=jnp.float32
    )
    in_terms = lax.dot_general(
        normed_all, hidden_grad, (((0,), (0,)), ((), ())), preferred_element_type=jnp.float32
    )
    grad_w2 = (scatter_split(out_terms_t) * scale).T
    grad_w1 = scatter_split(in_terms) * scale
    normed_grad = lax.psum_scatter(
        lax.dot_general(
            hidden_grad, w_in_cols, (((1,), (1,)), ((), ())), preferred_element_type=jnp.float32
        ),
        "cols",
        scatter_dimension=0,
        tiled=True,
    )
    gain_applied = (
        normed_grad.reshape(images, tile_rows, tile_cols, channel_total) * layer_norm_gain
    )
    convolution_gradient = inverse_deviation * (
        gain_applied
        - jnp.mean(gain_applied, axis=-1, keepdims=True)
        - standardized_input * jnp.mean(gain_applied * standardized_input, axis=-1, keepdims=True)
    )
    grad_t = to_tiles(convolution_gradient)
    kernel_rows = []
    for r in range(kernel_size):
        row_terms = []
        for s in range(kernel_size):
            term = jnp.sum(
                grad_t * padded[r : r + tile_rows, s : s + tile_cols].astype(jnp.float32),
                axis=(0, 1),
            )
            row_terms.append(term.reshape(images, channel_total).sum(axis=0))
        kernel_rows.append(jnp.stack(row_terms))
    grad_kernel = jnp.stack(kernel_rows).reshape(kernel_size * kernel_size * channel_total)
    col_order = tuple(range(col_bits))
    row_order = (0, 1, 3, 2, 4)[:row_bits]
    pieces = 1 << (col_bits + row_bits)
    grad_kernel = grad_kernel.reshape(pieces, -1)
    grad_kernel = scatter_rows(grad_kernel, "cols", col_order)
    grad_kernel = scatter_rows(grad_kernel, "rows", row_order)
    grad_kernel = gather_rows(grad_kernel, "rows", row_order[::-1])
    grad_kernel = gather_rows(grad_kernel, "cols", col_order[::-1])
    grad_kernel = grad_kernel.reshape(kernel_size, kernel_size, channel_total) * scale
    grad_pad = with_halo(grad_t, (("rows", 0), ("cols", 1)), kernel_reach)
    total = to_tiles(out_grad).astype(jnp.float32)
    for r in range(kernel_size):
        for s in range(kernel_size):
            row_from = 2 * kernel_reach - r
            col_from = 2 * kernel_reach - s
            total = (
                total
                + taps[r, s]
                * grad_pad[row_from : row_from + tile_rows, col_from : col_from + tile_cols]
            )
    total = from_tiles(total)
    input_grad = total.astype(jnp.bfloat16)
    return (input_grad, grad_w1, grad_w2, grad_kernel)


def solution(mesh):
    return jax.shard_map(
        local,
        mesh=mesh,
        in_specs=(
            P(None, "rows", "cols", None),
            P(None, ("rows", "cols"), None),
            P(),
            P(),
            P("rows", "cols"),
            P("cols", "rows"),
            P(),
        ),
        out_specs=(P(None, "rows", "cols", None), P("rows", "cols"), P("cols", "rows"), P()),
        check_vma=False,
    )
```

profile of v0, /device:TPU:1, one launch (start us, length us, event | category | flops | bytes accessed | tf_op | source)
XLA Modules:
  0.0 544.7 jit_solution(7361857078308796044)
XLA Ops:
  8.1 3.8 collective-permute-start.12
  19.9 5.0 collective-permute-start.17
  32.6 6.3 %collective-permute-start.14 = (bf16[192,512]{1,0:T(8,128)(2,1)S(1)}, bf16[192,512]{1,0:T(8,128)(2,1)S(1)}, u32[]{:S(2)}, u32[]{:S(2)}) collective-permute-start(bf16[192,512]{1,0:T(8,128)(2,1)S(1)} %fusion.193), channel_id=1, source_target_pairs={{0,8},{4,12},{8,0},{12,4},{16,24},{20,28},{24,16},{28,20},{32,40},... | collective-permute-start | bytes 589832 | tf_op jit(solution)/shard_map/ppermute | solution.py:22
  39.2 6.3 %collective-permute-start.9 = (bf16[192,512]{1,0:T(8,128)(2,1)S(1)}, bf16[192,512]{1,0:T(8,128)(2,1)S(1)}, u32[]{:S(2)}, u32[]{:S(2)}) collective-permute-start(bf16[192,512]{1,0:T(8,128)(2,1)S(1)} %fusion.195), channel_id=1, source_target_pairs={{0,4},{4,0},{8,12},{12,8},{16,20},{20,16},{24,28},{28,24},{32,36},... | collective-permute-start | bytes 589832 | tf_op jit(solution)/shard_map/ppermute | solution.py:22
  64.9 7.7 %collective-permute-start.19 = (bf16[10,3,24,128]{3,1,2,0:T(4,128)(2,1)}, bf16[10,3,24,128]{3,1,2,0:T(4,128)(2,1)S(1)}, u32[]{:S(2)}, u32[]{:S(2)}) collective-permute-start(bf16[10,3,24,128]{3,1,2,0:T(4,128)(2,1)} %get-tuple-element.71), channel_id=1, source_target_pairs={{0,1},{1,2},{2,3},{4,5},{5,6},{6,7},{8,9},{9,10},{10,11},{12,13},{... | collective-permute-start | bytes 552968 | tf_op jit(solution)/shard_map/ppermute | solution.py:14
  87.4 5.7 %collective-permute-done.11 = bf16[768,512]{1,0:T(8,128)(2,1)} collective-permute-done((bf16[768,512]{1,0:T(8,128)(2,1)}, bf16[768,512]{1,0:T(8,128)(2,1)}, u32[]{:S(2)}, u32[]{:S(2)}) %collective-permute-start.11) | collective-permute-done | bytes 786464 | tf_op jit(solution)/shard_map/ppermute | solution.py:22
  103.0 13.4 %fusion.79 = f32[4,32,24,128]{3,1,2,0:T(8,128)} fusion(f32[24,128]{1,0:T(8,128)S(1)} %bitcast.290, f32[24,128]{1,0:T(8,128)S(1)} %bitcast.292, f32[24,128]{1,0:T(8,128)S(1)} %bitcast.294, f32[24,128]{1,0:T(8,128)S(1)} %bitcast.296, f32[24,128]{1,0:T(8,128)S(1)} %bitcast.298, f32[24,128]{1,0:T(8,128)S(1)} %bitcast.300, f32[24,128]{1,0:T(8,128)S(1)} %bitcast.302, ...), kind=kLoop, calls=%fused_computation.202 | loop fusion | flops 57409536 | bytes 40710144 | tf_op jit(solution)/shard_map/add | solution.py:137
  125.4 11.0 %all-gather.3.cloned.1.call-start = ((), (), s32[]{:S(2)}) async-start(), calls=%async_computation.1 | async-start | bytes 3932160 | tf_op jit(solution)/shard_map/all_gather | solution.py:117
  139.4 5.2 collective-permute-start
  144.7 7.9 %collective-permute-done.1 = bf16[2,16,6144]{2,1,0:T(8,128)(2,1)S(1)} collective-permute-done((bf16[2,16,6144]{2,1,0:T(8,128)(2,1)}, bf16[2,16,6144]{2,1,0:T(8,128)(2,1)S(1)}, u32[]{:S(2)}, u32[]{:S(2)}) %collective-permute-start.1) | collective-permute-done | bytes 393248 | tf_op jit(solution)/shard_map/ppermute | solution.py:103
  152.6 16.6 %collective-permute-done = bf16[2,16,6144]{2,1,0:T(8,128)(2,1)S(1)} collective-permute-done((bf16[2,16,6144]{2,1,0:T(8,128)(2,1)}, bf16[2,16,6144]{2,1,0:T(8,128)(2,1)S(1)}, u32[]{:S(2)}, u32[]{:S(2)}) %collective-permute-start) | collective-permute-done | bytes 393248 | tf_op jit(solution)/shard_map/ppermute | solution.py:102
  182.7 6.9 %fusion.229 = f32[1024,768]{1,0:T(8,128)} fusion(bf16[1024,1536]{1,0:T(8,128)(2,1)} %all-gather.5.cloned.1.call-done, bf16[1536,768]{1,0:T(8,128)(2,1)} %get-tuple-element.9), kind=kOutput, calls=%fused_computation.560 | convolution fusion | flops 2415919104 | bytes 8650752 | tf_op jit(solution)/shard_map/dot_general | solution.py:152
  189.6 24.5 %all-gather.3.cloned.1.call-done = bf16[1024,1536]{1,0:T(8,128)(2,1)} async-done(((bf16[256,1536]{1,0:T(8,128)(2,1)}), bf16[1024,1536]{1,0:T(8,128)(2,1)}) %all-gather.3.cloned.1.call-update) | async-done | bytes 3145744 | tf_op jit(solution)/shard_map/all_gather | solution.py:117
  214.1 6.8 %fusion.5 = bf16[1024,768]{1,0:T(8,128)(2,1)S(1)} fusion(f32[1024,768]{1,0:T(8,128)} %fusion.229, bf16[1024,1536]{1,0:T(8,128)(2,1)} %all-gather.3.cloned.1.call-done, bf16[1536,768]{1,0:T(8,128)(2,1)} %get-tuple-element.8), kind=kOutput, calls=%fused_computation.16 | convolution fusion | flops 2423783424 | bytes 10223616 | tf_op jit(solution)/shard_map/dot_general | solution.py:155
  222.1 4.6 fusion.230
  233.6 5.3 fusion.109
  249.5 12.6 %collective-permute-done.40 = f32[768,256]{1,0:T(8,128)S(1)} collective-permute-done((f32[768,256]{1,0:T(8,128)S(1)}, f32[768,256]{1,0:T(8,128)S(1)}, u32[]{:S(2)}, u32[]{:S(2)}) %collective-permute-start.40) | collective-permute-done | bytes 786464 | tf_op jit(solution)/shard_map/ppermute | solution.py:22
  265.0 30.8 %collective-permute-done.25 = f32[768,256]{1,0:T(8,128)S(1)} collective-permute-done((f32[768,256]{1,0:T(8,128)S(1)}, f32[768,256]{1,0:T(8,128)S(1)}, u32[]{:S(2)}, u32[]{:S(2)}) %collective-permute-start.25) | collective-permute-done | bytes 786464 | tf_op jit(solution)/shard_map/ppermute | solution.py:22
  300.3 12.4 %collective-permute-done.51 = f32[384,256]{1,0:T(8,128)S(1)} collective-permute-done((f32[384,256]{1,0:T(8,128)S(1)}, f32[384,256]{1,0:T(8,128)S(1)}, u32[]{:S(2)}, u32[]{:S(2)}) %collective-permute-start.51) | collective-permute-done | bytes 393248 | tf_op jit(solution)/shard_map/ppermute | solution.py:22
  316.5 9.4 %collective-permute-done.36 = f32[384,256]{1,0:T(8,128)S(1)} collective-permute-done((f32[384,256]{1,0:T(8,128)S(1)}, f32[384,256]{1,0:T(8,128)S(1)}, u32[]{:S(2)}, u32[]{:S(2)}) %collective-permute-start.36) | collective-permute-done | bytes 393248 | tf_op jit(solution)/shard_map/ppermute | solution.py:22
  360.8 3.7 fusion.43
  364.4 5.0 fusion.84
  369.4 4.9 fusion.102
  397.1 6.1 %collective-permute-start.55 = (f32[64,588]{1,0:T(8,128)S(1)}, f32[64,588]{1,0:T(8,128)S(1)}, u32[]{:S(2)}, u32[]{:S(2)}) collective-permute-start(f32[64,588]{1,0:T(8,128)S(1)} %constant_dynamic-slice_fusion.14), channel_id=1, source_target_pairs={{0,1},{1,0},{2,3},{3,2},{4,5},{5,4},{6,7},{7,6},{8,9},{9,8},{10,11... | collective-permute-start | bytes 451592 | tf_op jit(solution)/shard_map/ppermute | solution.py:22
  405.1 4.3 collective-permute-done.56
  434.3 5.4 collective-permute-start.21
  447.3 15.8 %collective-permute-start.65 = (f32[8,588]{1,0:T(8,128)S(1)}, f32[8,588]{1,0:T(8,128)S(1)}, u32[]{:S(2)}, u32[]{:S(2)}) collective-permute-start(f32[8,588]{1,0:T(8,128)S(1)} %fusion.213), channel_id=1, source_target_pairs={{0,8},{4,12},{8,0},{12,4},{16,24},{20,28},{24,16},{28,20},{32,40},... | collective-permute-start | bytes 56456 | tf_op jit(solution)/shard_map/ppermute | solution.py:22
  464.6 4.8 collective-permute-start.66
  470.0 19.7 %collective-permute-done.66 = f32[16,588]{1,0:T(8,128)S(1)} collective-permute-done((f32[16,588]{1,0:T(8,128)S(1)}, f32[16,588]{1,0:T(8,128)S(1)}, u32[]{:S(2)}, u32[]{:S(2)}) %collective-permute-start.66) | collective-permute-done | bytes 37664 | tf_op jit(solution)/shard_map/ppermute | solution.py:22
  495.9 4.4 collective-permute-start.24
  506.1 5.6 %pad_maximum_fusion = (f32[10,35,24,128]{3,1,2,0:T(8,128)S(1)}, f32[10,35,24,128]{3,1,2,0:T(8,128)}) fusion(f32[10,3,24,128]{3,1,2,0:T(4,128)} %copy-done.8, f32[3,32,24,128]{3,1,2,0:T(8,128)} %copy-done.3, f32[4,32,24,128]{3,1,2,0:T(8,128)} %bitcast.171, f32[3,32,24,128]{3,1,2,0:T(8,128)} %collective-permute-done.21, f32[10,3,24,128]{3,1,2,0:T(4,128)} %collective-permute-done.24), kind=kLoop, calls=%fused_computation | loop fusion | flops 6451200 | bytes 13271040 | tf_op jit(solution)/shard_map/concatenate | solution.py:16
  511.8 23.2 %fusion.173 = bf16[4,32,24,128]{3,1,2,0:T(8,128)(2,1)} fusion(f32[10,35,24,128]{3,1,2,0:T(8,128)} %get-tuple-element.68, f32[4,32,24,128]{3,1,2,0:T(8,128)} %bitcast.172, f32[3,32,24,128]{3,1,2,0:T(8,128)} %collective-permute-done.21, f32[10,35,24,128]{3,1,2,0:T(8,128)S(1)} %get-tuple-element.67, f32[3,32,24,128]{3,1,2,0:T(8,128)} %copy-done.3, ...), kind=kLoop, calls=%fused_computation.346 | loop fusion | flops 41287680 | bytes 72953856 | tf_op jit(solution)/shard_map/convert_element_type | solution.py:216
  (659 shorter events, 222.3 us)
Async XLA Ops:
  7.2 175.6 %all-gather.5.cloned.1.call-start = ((), (), s32[]{:S(2)}) async-start(), calls=%async_computation.2 | async-start | bytes 3932160 | tf_op jit(solution)/shard_map/all_gather | solution.py:151
  8.1 19.0 %collective-permute-start.12 = (bf16[48,512]{1,0:T(8,128)(2,1)S(1)}, bf16[48,512]{1,0:T(8,128)(2,1)S(1)}, u32[]{:S(2)}, u32[]{:S(2)}) collective-permute-start(bf16[48,512]{1,0:T(8,128)(2,1)S(1)} %get-tuple-element.130), channel_id=1, source_target_pairs={{0,64},{4,68},{8,72},{12,76},{16,80},{20,84},{24,88},{28,92},{32,9... | collective-permute-start | bytes 147464 | tf_op jit(solution)/shard_map/ppermute | solution.py:22
  17.7 45.1 %collective-permute-start.18 = (bf16[3,32,24,128]{3,1,2,0:T(8,128)(2,1)}, bf16[3,32,24,128]{3,1,2,0:T(8,128)(2,1)S(1)}, u32[]{:S(2)}, u32[]{:S(2)}) collective-permute-start(bf16[3,32,24,128]{3,1,2,0:T(8,128)(2,1)} %bitcast.24), channel_id=1, source_target_pairs={{4,0},{8,4},{12,8},{16,12},{20,16},{24,20},{28,24},{32,28},{36,32}... | collective-permute-start | bytes 1769480 | tf_op jit(solution)/shard_map/ppermute | solution.py:15
  19.9 42.9 %collective-permute-start.17 = (bf16[3,32,24,128]{3,1,2,0:T(8,128)(2,1)}, bf16[3,32,24,128]{3,1,2,0:T(8,128)(2,1)}, u32[]{:S(2)}, u32[]{:S(2)}) collective-permute-start(bf16[3,32,24,128]{3,1,2,0:T(8,128)(2,1)} %bitcast.22), channel_id=1, source_target_pairs={{0,4},{4,8},{8,12},{12,16},{16,20},{20,24},{24,28},{28,32},{32,36}... | collective-permute-start | bytes 1769480 | tf_op jit(solution)/shard_map/ppermute | solution.py:14
  26.0 19.5 %collective-permute-start.3 = (bf16[96,512]{1,0:T(8,128)(2,1)S(1)}, bf16[96,512]{1,0:T(8,128)(2,1)S(1)}, u32[]{:S(2)}, u32[]{:S(2)}) collective-permute-start(bf16[96,512]{1,0:T(8,128)(2,1)S(1)} %fusion.206), channel_id=1, source_target_pairs={{0,16},{4,20},{8,24},{12,28},{16,0},{20,4},{24,8},{28,12},{32,48},... | collective-permute-start | bytes 294920 | tf_op jit(solution)/shard_map/ppermute | solution.py:22
  53.7 20.8 %collective-permute-start.10 = (bf16[384,512]{1,0:T(8,128)(2,1)}, bf16[384,512]{1,0:T(8,128)(2,1)}, u32[]{:S(2)}, u32[]{:S(2)}) collective-permute-start(bf16[384,512]{1,0:T(8,128)(2,1)} %fusion.186), channel_id=1, source_target_pairs={{0,32},{4,36},{8,40},{12,44},{16,48},{20,52},{24,56},{28,60},{32,0... | collective-permute-start | bytes 1179656 | tf_op jit(solution)/shard_map/ppermute | solution.py:22
  57.5 20.8 %collective-permute-start.5 = (bf16[384,512]{1,0:T(8,128)(2,1)S(1)}, bf16[384,512]{1,0:T(8,128)(2,1)S(1)}, u32[]{:S(2)}, u32[]{:S(2)}) collective-permute-start(bf16[384,512]{1,0:T(8,128)(2,1)S(1)} %fusion.188), channel_id=1, source_target_pairs={{0,8},{4,12},{8,0},{12,4},{16,24},{20,28},{24,16},{28,20},{32,40},... | collective-permute-start | bytes 1179656 | tf_op jit(solution)/shard_map/ppermute | solution.py:22
  61.5 23.0 %collective-permute-start.16 = (bf16[768,512]{1,0:T(8,128)(2,1)}, bf16[768,512]{1,0:T(8,128)(2,1)}, u32[]{:S(2)}, u32[]{:S(2)}) collective-permute-start(bf16[768,512]{1,0:T(8,128)(2,1)} %fusion.175), channel_id=1, source_target_pairs={{0,32},{4,36},{8,40},{12,44},{16,48},{20,52},{24,56},{28,60},{32,0... | collective-permute-start | bytes 2359304 | tf_op jit(solution)/shard_map/ppermute | solution.py:22
  125.4 88.7 %all-gather.3.cloned.1.call-start = ((), (), s32[]{:S(2)}) async-start(), calls=%async_computation.1 | async-start | bytes 3932160 | tf_op jit(solution)/shard_map/all_gather | solution.py:117
  139.4 29.8 %collective-permute-start = (bf16[2,16,6144]{2,1,0:T(8,128)(2,1)}, bf16[2,16,6144]{2,1,0:T(8,128)(2,1)S(1)}, u32[]{:S(2)}, u32[]{:S(2)}) collective-permute-start(bf16[2,16,6144]{2,1,0:T(8,128)(2,1)} %get-tuple-element.80), channel_id=1, source_target_pairs={{0,0},{1,2},{2,1},{3,3},{4,4},{5,6},{6,5},{7,7},{8,8},{9,10},{10,9... | collective-permute-start | bytes 1179656 | tf_op jit(solution)/shard_map/ppermute | solution.py:102
  182.7 163.8 %reduce-scatter.2.cloned.1.call-start = ((), (), s32[]{:S(2)}) async-start(), calls=%async_computation.3 | async-start | bytes 7864320 | tf_op jit(solution)/shard_map/reduce_scatter | solution.py:167
  239.7 22.4 %collective-permute-start.40 = (f32[768,256]{1,0:T(8,128)S(1)}, f32[768,256]{1,0:T(8,128)S(1)}, u32[]{:S(2)}, u32[]{:S(2)}) collective-permute-start(f32[768,256]{1,0:T(8,128)S(1)} %constant_dynamic-slice_fusion.29), channel_id=1, source_target_pairs={{0,4},{4,0},{8,12},{12,8},{16,20},{20,16},{24,28},{28,24},{32,36},... | collective-permute-start | bytes 2359304 | tf_op jit(solution)/shard_map/ppermute | solution.py:22
  240.0 24.2 %collective-permute-start.50 = (f32[768,256]{1,0:T(8,128)S(1)}, f32[768,256]{1,0:T(8,128)S(1)}, u32[]{:S(2)}, u32[]{:S(2)}) collective-permute-start(f32[768,256]{1,0:T(8,128)S(1)} %constant_dynamic-slice_fusion.19), channel_id=1, source_target_pairs={{0,32},{4,36},{8,40},{12,44},{16,48},{20,52},{24,56},{28,60},{32,0... | collective-permute-start | bytes 2359304 | tf_op jit(solution)/shard_map/ppermute | solution.py:22
  241.6 22.8 %collective-permute-start.45 = (f32[768,256]{1,0:T(8,128)S(1)}, f32[768,256]{1,0:T(8,128)S(1)}, u32[]{:S(2)}, u32[]{:S(2)}) collective-permute-start(f32[768,256]{1,0:T(8,128)S(1)} %constant_dynamic-slice_fusion.24), channel_id=1, source_target_pairs={{0,8},{4,12},{8,0},{12,4},{16,24},{20,28},{24,16},{28,20},{32,40},... | collective-permute-start | bytes 2359304 | tf_op jit(solution)/shard_map/ppermute | solution.py:22
  247.4 48.5 %collective-permute-start.25 = (f32[768,256]{1,0:T(8,128)S(1)}, f32[768,256]{1,0:T(8,128)S(1)}, u32[]{:S(2)}, u32[]{:S(2)}) collective-permute-start(f32[768,256]{1,0:T(8,128)S(1)} %constant_dynamic-slice_fusion.44), channel_id=1, source_target_pairs={{0,4},{4,0},{8,12},{12,8},{16,20},{20,16},{24,28},{28,24},{32,36},... | collective-permute-start | bytes 2359304 | tf_op jit(solution)/shard_map/ppermute | solution.py:22
  249.0 48.9 %collective-permute-start.35 = (f32[768,256]{1,0:T(8,128)S(1)}, f32[768,256]{1,0:T(8,128)S(1)}, u32[]{:S(2)}, u32[]{:S(2)}) collective-permute-start(f32[768,256]{1,0:T(8,128)S(1)} %constant_dynamic-slice_fusion.34), channel_id=1, source_target_pairs={{0,32},{4,36},{8,40},{12,44},{16,48},{20,52},{24,56},{28,60},{32,0... | collective-permute-start | bytes 2359304 | tf_op jit(solution)/shard_map/ppermute | solution.py:22
  262.2 37.2 %collective-permute-start.30 = (f32[768,256]{1,0:T(8,128)S(1)}, f32[768,256]{1,0:T(8,128)S(1)}, u32[]{:S(2)}, u32[]{:S(2)}) collective-permute-start(f32[768,256]{1,0:T(8,128)S(1)} %constant_dynamic-slice_fusion.39), channel_id=1, source_target_pairs={{0,8},{4,12},{8,0},{12,4},{16,24},{20,28},{24,16},{28,20},{32,40},... | collective-permute-start | bytes 2359304 | tf_op jit(solution)/shard_map/ppermute | solution.py:22
  264.2 35.7 %collective-permute-start.41 = (f32[384,256]{1,0:T(8,128)S(1)}, f32[384,256]{1,0:T(8,128)S(1)}, u32[]{:S(2)}, u32[]{:S(2)}) collective-permute-start(f32[384,256]{1,0:T(8,128)S(1)} %constant_dynamic-slice_fusion.28), channel_id=1, source_target_pairs={{0,8},{4,12},{8,0},{12,4},{16,24},{20,28},{24,16},{28,20},{32,40},... | collective-permute-start | bytes 1179656 | tf_op jit(solution)/shard_map/ppermute | solution.py:22
  264.4 48.3 %collective-permute-start.51 = (f32[384,256]{1,0:T(8,128)S(1)}, f32[384,256]{1,0:T(8,128)S(1)}, u32[]{:S(2)}, u32[]{:S(2)}) collective-permute-start(f32[384,256]{1,0:T(8,128)S(1)} %constant_dynamic-slice_fusion.18), channel_id=1, source_target_pairs={{0,4},{4,0},{8,12},{12,8},{16,20},{20,16},{24,28},{28,24},{32,36},... | collective-permute-start | bytes 1179656 | tf_op jit(solution)/shard_map/ppermute | solution.py:22
  299.3 26.5 %collective-permute-start.36 = (f32[384,256]{1,0:T(8,128)S(1)}, f32[384,256]{1,0:T(8,128)S(1)}, u32[]{:S(2)}, u32[]{:S(2)}) collective-permute-start(f32[384,256]{1,0:T(8,128)S(1)} %constant_dynamic-slice_fusion.33), channel_id=1, source_target_pairs={{0,4},{4,0},{8,12},{12,8},{16,20},{20,16},{24,28},{28,24},{32,36},... | collective-permute-start | bytes 1179656 | tf_op jit(solution)/shard_map/ppermute | solution.py:22
  299.8 27.6 %collective-permute-start.31 = (f32[384,256]{1,0:T(8,128)S(1)}, f32[384,256]{1,0:T(8,128)S(1)}, u32[]{:S(2)}, u32[]{:S(2)}) collective-permute-start(f32[384,256]{1,0:T(8,128)S(1)} %constant_dynamic-slice_fusion.38), channel_id=1, source_target_pairs={{0,32},{4,36},{8,40},{12,44},{16,48},{20,52},{24,56},{28,60},{32,0... | collective-permute-start | bytes 1179656 | tf_op jit(solution)/shard_map/ppermute | solution.py:22
  337.6 59.4 %collective-permute-start.38 = (f32[96,256]{1,0:T(8,128)S(1)}, f32[96,256]{1,0:T(8,128)}, u32[]{:S(2)}, u32[]{:S(2)}) collective-permute-start(f32[96,256]{1,0:T(8,128)S(1)} %constant_dynamic-slice_fusion.31), channel_id=1, source_target_pairs={{0,16},{4,20},{8,24},{12,28},{16,0},{20,4},{24,8},{28,12},{32,48},... | collective-permute-start | bytes 294920 | tf_op jit(solution)/shard_map/ppermute | solution.py:22
  339.3 71.7 %collective-permute-start.33 = (f32[96,256]{1,0:T(8,128)S(1)}, f32[96,256]{1,0:T(8,128)S(1)}, u32[]{:S(2)}, u32[]{:S(2)}) collective-permute-start(f32[96,256]{1,0:T(8,128)S(1)} %constant_dynamic-slice_fusion.36), channel_id=1, source_target_pairs={{0,64},{4,68},{8,72},{12,76},{16,80},{20,84},{24,88},{28,92},{32,9... | collective-permute-start | bytes 294920 | tf_op jit(solution)/shard_map/ppermute | solution.py:22
  340.3 80.7 %collective-permute-start.44 = (f32[48,256]{1,0:T(8,128)}, f32[48,256]{1,0:T(8,128)}, u32[]{:S(2)}, u32[]{:S(2)}) collective-permute-start(f32[48,256]{1,0:T(8,128)} %constant_dynamic-slice_fusion.25), channel_id=1, source_target_pairs={{0,64},{4,68},{8,72},{12,76},{16,80},{20,84},{24,88},{28,92},{32,9... | collective-permute-start | bytes 147464 | tf_op jit(solution)/shard_map/ppermute | solution.py:22
  343.7 83.0 %collective-permute-start.54 = (f32[48,256]{1,0:T(8,128)}, f32[48,256]{1,0:T(8,128)}, u32[]{:S(2)}, u32[]{:S(2)}) collective-permute-start(f32[48,256]{1,0:T(8,128)} %constant_dynamic-slice_fusion.15), channel_id=1, source_target_pairs={{0,64},{4,68},{8,72},{12,76},{16,80},{20,84},{24,88},{28,92},{32,9... | collective-permute-start | bytes 147464 | tf_op jit(solution)/shard_map/ppermute | solution.py:22
  344.5 118.6 %collective-permute-start.49 = (f32[48,256]{1,0:T(8,128)}, f32[48,256]{1,0:T(8,128)}, u32[]{:S(2)}, u32[]{:S(2)}) collective-permute-start(f32[48,256]{1,0:T(8,128)} %constant_dynamic-slice_fusion.20), channel_id=1, source_target_pairs={{0,16},{4,20},{8,24},{12,28},{16,0},{20,4},{24,8},{28,12},{32,48},... | collective-permute-start | bytes 147464 | tf_op jit(solution)/shard_map/ppermute | solution.py:22
  409.4 30.3 %collective-permute-start.29 = (f32[48,256]{1,0:T(8,128)}, f32[48,256]{1,0:T(8,128)}, u32[]{:S(2)}, u32[]{:S(2)}) collective-permute-start(f32[48,256]{1,0:T(8,128)} %constant_dynamic-slice_fusion.40), channel_id=1, source_target_pairs={{0,64},{4,68},{8,72},{12,76},{16,80},{20,84},{24,88},{28,92},{32,9... | collective-permute-start | bytes 147464 | tf_op jit(solution)/shard_map/ppermute | solution.py:22
  419.5 24.8 %collective-permute-start.39 = (f32[48,256]{1,0:T(8,128)S(1)}, f32[48,256]{1,0:T(8,128)S(1)}, u32[]{:S(2)}, u32[]{:S(2)}) collective-permute-start(f32[48,256]{1,0:T(8,128)S(1)} %constant_dynamic-slice_fusion.30), channel_id=1, source_target_pairs={{0,64},{4,68},{8,72},{12,76},{16,80},{20,84},{24,88},{28,92},{32,9... | collective-permute-start | bytes 147464 | tf_op jit(solution)/shard_map/ppermute | solution.py:22
  433.0 57.7 %collective-permute-start.22 = (f32[3,32,24,128]{3,1,2,0:T(8,128)}, f32[3,32,24,128]{3,1,2,0:T(8,128)S(1)}, u32[]{:S(2)}, u32[]{:S(2)}) collective-permute-start(f32[3,32,24,128]{3,1,2,0:T(8,128)} %bitcast.80), channel_id=1, source_target_pairs={{4,0},{8,4},{12,8},{16,12},{20,16},{24,20},{28,24},{32,28},{36,32}... | collective-permute-start | bytes 3538952 | tf_op jit(solution)/shard_map/ppermute | solution.py:15
  434.3 56.4 %collective-permute-start.21 = (f32[3,32,24,128]{3,1,2,0:T(8,128)}, f32[3,32,24,128]{3,1,2,0:T(8,128)}, u32[]{:S(2)}, u32[]{:S(2)}) collective-permute-start(f32[3,32,24,128]{3,1,2,0:T(8,128)} %bitcast.78), channel_id=1, source_target_pairs={{0,4},{4,8},{8,12},{12,16},{16,20},{20,24},{24,28},{28,32},{32,36}... | collective-permute-start | bytes 3538952 | tf_op jit(solution)/shard_map/ppermute | solution.py:14
  443.8 25.5 %collective-permute-start.34 = (f32[48,256]{1,0:T(8,128)S(1)}, f32[48,256]{1,0:T(8,128)S(1)}, u32[]{:S(2)}, u32[]{:S(2)}) collective-permute-start(f32[48,256]{1,0:T(8,128)S(1)} %constant_dynamic-slice_fusion.35), channel_id=1, source_target_pairs={{0,16},{4,20},{8,24},{12,28},{16,0},{20,4},{24,8},{28,12},{32,48},... | collective-permute-start | bytes 147464 | tf_op jit(solution)/shard_map/ppermute | solution.py:22
  464.6 25.1 %collective-permute-start.66 = (f32[16,588]{1,0:T(8,128)S(1)}, f32[16,588]{1,0:T(8,128)S(1)}, u32[]{:S(2)}, u32[]{:S(2)}) collective-permute-start(f32[16,588]{1,0:T(8,128)S(1)} %fusion.210), channel_id=1, source_target_pairs={{0,4},{4,0},{8,12},{12,8},{16,20},{20,16},{24,28},{28,24},{32,36},... | collective-permute-start | bytes 112904 | tf_op jit(solution)/shard_map/ppermute | solution.py:22
  (145 other events, 1374.0 us)
Sparse Core Ops, SparseCore 0:
  125.5 45.2 all-gather.4
  182.8 31.2 all-gather.2
  226.9 98.5 reduce-scatter.1
where the time goes:
time: 548 us; the launch traced here: 545 us
  waiting for transfers between devices  167 us (30%)
  starting transfers between devices  151 us (28%)
  other arithmetic  114 us (21%)
  local copies, waits for them, and re-layouts  68.9 us (13%)
  matrix products  26.2 us (5%)
  between operations  17.3 us (3%)
    ppermute x59, waiting for transfers between devices, swap_with(): return lax.ppermute(value, axis, [(i, i ^ 1 << bit) for i in range(peers)])  116 us
    ppermute x59, starting transfers between devices, swap_with(): return lax.ppermute(value, axis, [(i, i ^ 1 << bit) for i in range(peers)])  103 us
    all_gather x1, waiting for transfers between devices, local(): branch_all = lax.all_gather(branch_grad, 'cols', axis=0, tiled=True)  24.5 us
    convert_element_type x1, other arithmetic, local(): input_grad = total.astype(jnp.bfloat16)  23.2 us
    ppermute x4, starting transfers between devices, with_halo(): before = lax.ppermute(last, axis, up)  22.5 us
    concatenate x21, other arithmetic, gather_rows(): both = jnp.concatenate([value, other, value], axis=0)  21.7 us
    reshape x49, local copies, waits for them, and re-layouts, local(): row_terms.append(term.reshape(images, channel_total).sum(axis=0))  19.1 us
    ppermute x1, waiting for transfers between devices, local(): lax.ppermute(send_a, 'cols', [(s, 2 * (s % 2) + s // 2) for s in range(n_...  16.6 us
  transfers between devices with their start and end apart: 72, of which 24 were waited for; matrix products, arithmetic and copies ran while one was open for 25% of the time, Pallas kernels for 0%

commit v1 on v0

--- a/solution.py
+++ b/solution.py
@@ -38,7 +38,7 @@
     return value.reshape((block << n,) + rest)
 
 
-def scatter_rows(value, axis, order):
+def scatter_rows(value, axis, order, narrow_steps=0):
     me = lax.axis_index(axis)
     n = len(order)
     block = value.shape[0] >> n
@@ -46,12 +46,16 @@
     value = value.reshape((2,) * n + (block,) + rest)
     perm = [n - 1 - order[j] for j in range(n)]
     value = value.transpose(perm + list(range(n, value.ndim))).reshape((block << n,) + rest)
-    for bit in order:
+    for step, bit in enumerate(order):
         half = value.shape[0] // 2
         b = (me >> bit) & 1
         keep = lax.dynamic_slice_in_dim(value, b * half, half, axis=0)
         send = lax.dynamic_slice_in_dim(value, (1 - b) * half, half, axis=0)
-        value = keep + swap_with(send, axis, bit)
+        if step < narrow_steps:
+            got = swap_with(send.astype(jnp.bfloat16), axis, bit).astype(value.dtype)
+        else:
+            got = swap_with(send, axis, bit)
+        value = keep + got
     return value
 
 
@@ -63,7 +67,7 @@
     third = value.shape[1] // 3
     return jnp.concatenate(
         [
-            scatter_rows(value[:, i * third : (i + 1) * third], "rows", order)
+            scatter_rows(value[:, i * third : (i + 1) * third], "rows", order, 2)
             for i, order in enumerate(SCATTER_ORDERS)
         ],
         axis=1,
@@ -114,7 +118,6 @@
         .astype(jnp.bfloat16)
         .reshape(pixel_total, channel_total)
     )
-    branch_all = lax.all_gather(branch_grad, "cols", axis=0, tiled=True)
     lane = 128
     groups = channel_total // lane
 
@@ -130,7 +133,10 @@
         conv_kernel.reshape(kernel_size, kernel_size, 1, groups, lane), (1, 1, images, 1, 1)
     ).reshape(kernel_size, kernel_size, images * groups, lane)
     padded = with_halo(to_tiles(block_input), (("rows", 0), ("cols", 1)), kernel_reach)
-    w_in_cols, w_out_cols_t, padded = lax.optimization_barrier((w_in_cols, w_out_cols_t, padded))
+    w_in_cols, w_out_cols_t, branch_grad, padded = lax.optimization_barrier(
+        (w_in_cols, w_out_cols_t, branch_grad, padded)
+    )
+    branch_all = lax.all_gather(branch_grad, "cols", axis=0, tiled=True)
     conv_t = jnp.zeros((tile_rows, tile_cols, images * groups, lane), jnp.float32)
     for r in range(kernel_size):
         for s in range(kernel_size):

time: 548 us -> 522 us (0.953)
  the two profiles are of different devices: /device:TPU:1 before, /device:TPU:102 now
where the time goes in v1:
time: 522 us; the launch traced here: 512 us
  waiting for transfers between devices  154 us (30%)
  starting transfers between devices  133 us (25%)
  other arithmetic  112 us (21%)
  local copies, waits for them, and re-layouts  68.1 us (13%)
  matrix products  25.7 us (5%)
  between operations  17.6 us (3%)
    ppermute x59, starting transfers between devices, swap_with(): return lax.ppermute(value, axis, [(i, i ^ 1 << bit) for i in range(peers)])  104 us
    ppermute x59, waiting for transfers between devices, swap_with(): return lax.ppermute(value, axis, [(i, i ^ 1 << bit) for i in range(peers)])  81.5 us
    all_gather x1, waiting for transfers between devices, local(): normed_all = lax.all_gather(norm_output, 'cols', axis=0, tiled=True)  33.2 us
    all_gather x1, waiting for transfers between devices, local(): branch_all = lax.all_gather(branch_grad, 'cols', axis=0, tiled=True)  26.7 us
    convert_element_type x1, other arithmetic, local(): input_grad = total.astype(jnp.bfloat16)  23.2 us
    concatenate x21, other arithmetic, gather_rows(): both = jnp.concatenate([value, other, value], axis=0)  22.6 us
    reshape x49, local copies, waits for them, and re-layouts, local(): row_terms.append(term.reshape(images, channel_total).sum(axis=0))  19.1 us
    reduce_sum x3, other arithmetic, local(): jnp.sum(grad_t * padded[r:r + tile_rows, s:s + tile_cols].astype(jnp.floa...  13.6 us
  transfers between devices with their start and end apart: 72, of which 30 were waited for; matrix products, arithmetic and copies ran while one was open for 25% of the time, Pallas kernels for 0%

profile of v1, /device:TPU:102, one launch (start us, length us, event | category | flops | bytes accessed | tf_op | source)
XLA Modules:
  0.0 511.7 jit_solution(14956117381436795844)
XLA Ops:
  8.1 3.3 collective-permute-start.12
  33.6 5.3 %collective-permute-done.13 = bf16[96,512]{1,0:T(8,128)(2,1)S(1)} collective-permute-done((bf16[96,512]{1,0:T(8,128)(2,1)S(1)}, bf16[96,512]{1,0:T(8,128)(2,1)S(1)}, u32[]{:S(2)}, u32[]{:S(2)}) %collective-permute-start.13) | collective-permute-done | bytes 98336 | tf_op jit(solution)/shard_map/ppermute | solution.py:22
  48.8 13.0 %collective-permute-start.9 = (bf16[192,512]{1,0:T(8,128)(2,1)S(1)}, bf16[192,512]{1,0:T(8,128)(2,1)S(1)}, u32[]{:S(2)}, u32[]{:S(2)}) collective-permute-start(bf16[192,512]{1,0:T(8,128)(2,1)S(1)} %fusion.195), channel_id=1, source_target_pairs={{0,4},{4,0},{8,12},{12,8},{16,20},{20,16},{24,28},{28,24},{32,36},... | collective-permute-start | bytes 589832 | tf_op jit(solution)/shard_map/ppermute | solution.py:22
  84.9 5.3 %collective-permute-start.20 = (bf16[10,3,24,128]{3,1,2,0:T(4,128)(2,1)S(1)}, bf16[10,3,24,128]{3,1,2,0:T(4,128)(2,1)}, u32[]{:S(2)}, u32[]{:S(2)}) collective-permute-start(bf16[10,3,24,128]{3,1,2,0:T(4,128)(2,1)S(1)} %get-tuple-element.74), channel_id=1, source_target_pairs={{1,0},{2,1},{3,2},{5,4},{6,5},{7,6},{9,8},{10,9},{11,10},{13,12},{... | collective-permute-start | bytes 552968 | tf_op jit(solution)/shard_map/ppermute | solution.py:15
  104.5 6.1 %collective-permute-done.16 = bf16[768,512]{1,0:T(8,128)(2,1)} collective-permute-done((bf16[768,512]{1,0:T(8,128)(2,1)}, bf16[768,512]{1,0:T(8,128)(2,1)}, u32[]{:S(2)}, u32[]{:S(2)}) %collective-permute-start.16) | collective-permute-done | bytes 786464 | tf_op jit(solution)/shard_map/ppermute | solution.py:22
  117.2 3.4 fusion.108
  123.8 13.4 %fusion.79 = f32[4,32,24,128]{3,1,2,0:T(8,128)} fusion(f32[24,128]{1,0:T(8,128)S(1)} %bitcast.288, f32[24,128]{1,0:T(8,128)S(1)} %bitcast.290, f32[24,128]{1,0:T(8,128)S(1)} %bitcast.292, f32[24,128]{1,0:T(8,128)S(1)} %bitcast.294, f32[24,128]{1,0:T(8,128)S(1)} %bitcast.296, f32[24,128]{1,0:T(8,128)S(1)} %bitcast.298, f32[24,128]{1,0:T(8,128)S(1)} %bitcast.300, ...), kind=kLoop, calls=%fused_computation.202 | loop fusion | flops 57409536 | bytes 40710144 | tf_op jit(solution)/shard_map/add | solution.py:143
  147.0 33.2 %all-gather.5.cloned.1.call-done = bf16[1024,1536]{1,0:T(8,128)(2,1)} async-done(((bf16[256,1536]{1,0:T(8,128)(2,1)}), bf16[1024,1536]{1,0:T(8,128)(2,1)}) %all-gather.5.cloned.1.call-update) | async-done | bytes 3145744 | tf_op jit(solution)/shard_map/all_gather | solution.py:157
  180.2 6.9 %fusion.229 = f32[1024,768]{1,0:T(8,128)} fusion(bf16[1024,1536]{1,0:T(8,128)(2,1)} %all-gather.5.cloned.1.call-done, bf16[1536,768]{1,0:T(8,128)(2,1)} %get-tuple-element.11), kind=kOutput, calls=%fused_computation.560 | convolution fusion | flops 2415919104 | bytes 8650752 | tf_op jit(solution)/shard_map/dot_general | solution.py:158
  187.0 26.7 %all-gather.3.cloned.1.call-done = bf16[1024,1536]{1,0:T(8,128)(2,1)} async-done(((bf16[256,1536]{1,0:T(8,128)(2,1)}), bf16[1024,1536]{1,0:T(8,128)(2,1)}) %all-gather.3.cloned.1.call-update) | async-done | bytes 3145744 | tf_op jit(solution)/shard_map/all_gather | solution.py:139
  213.7 6.8 %fusion.5 = bf16[1024,768]{1,0:T(8,128)(2,1)S(1)} fusion(f32[1024,768]{1,0:T(8,128)} %fusion.229, bf16[1024,1536]{1,0:T(8,128)(2,1)} %all-gather.3.cloned.1.call-done, bf16[1536,768]{1,0:T(8,128)(2,1)} %get-tuple-element.10), kind=kOutput, calls=%fused_computation.16 | convolution fusion | flops 2423783424 | bytes 10223616 | tf_op jit(solution)/shard_map/dot_general | solution.py:161
  221.8 4.6 fusion.230
  226.4 3.4 reshape.415
  229.8 3.4 copy.84
  233.2 4.7 fusion.109
  254.7 8.1 %collective-permute-done.25 = bf16[768,256]{1,0:T(8,128)(2,1)S(1)} collective-permute-done((bf16[768,256]{1,0:T(8,128)(2,1)S(1)}, bf16[768,256]{1,0:T(8,128)(2,1)S(1)}, u32[]{:S(2)}, u32[]{:S(2)}) %collective-permute-start.25) | collective-permute-done | bytes 393248 | tf_op jit(solution)/shard_map/ppermute | solution.py:22
  267.8 3.5 collective-permute-done.51
  274.0 5.7 %collective-permute-done.36 = bf16[384,256]{1,0:T(8,128)(2,1)S(1)} collective-permute-done((bf16[384,256]{1,0:T(8,128)(2,1)S(1)}, bf16[384,256]{1,0:T(8,128)(2,1)S(1)}, u32[]{:S(2)}, u32[]{:S(2)}) %collective-permute-start.36) | collective-permute-done | bytes 196640 | tf_op jit(solution)/shard_map/ppermute | solution.py:22
  283.7 4.4 collective-permute-done.47
  308.2 5.1 reduce-scatter.2.cloned.1.call-done
  327.5 3.7 fusion.43
  331.2 5.0 fusion.84
  336.2 4.9 fusion.102
  366.1 5.3 %collective-permute-done.56 = f32[32,588]{1,0:T(8,128)S(1)} collective-permute-done((f32[32,588]{1,0:T(8,128)S(1)}, f32[32,588]{1,0:T(8,128)S(1)}, u32[]{:S(2)}, u32[]{:S(2)}) %collective-permute-start.56) | collective-permute-done | bytes 75296 | tf_op jit(solution)/shard_map/ppermute | solution.py:22
  374.8 4.0 collective-permute-done.57
  404.4 6.9 %collective-permute-start.21 = (f32[3,32,24,128]{3,1,2,0:T(8,128)}, f32[3,32,24,128]{3,1,2,0:T(8,128)}, u32[]{:S(2)}, u32[]{:S(2)}) collective-permute-start(f32[3,32,24,128]{3,1,2,0:T(8,128)} %bitcast.78), channel_id=1, source_target_pairs={{0,4},{4,8},{8,12},{12,16},{16,20},{20,24},{24,28},{28,32},{32,36}... | collective-permute-start | bytes 3538952 | tf_op jit(solution)/shard_map/ppermute | solution.py:14
  412.3 4.3 collective-permute-done.63
  420.5 17.2 %collective-permute-start.65 = (f32[8,588]{1,0:T(8,128)S(1)}, f32[8,588]{1,0:T(8,128)S(1)}, u32[]{:S(2)}, u32[]{:S(2)}) collective-permute-start(f32[8,588]{1,0:T(8,128)S(1)} %fusion.213), channel_id=1, source_target_pairs={{0,8},{4,12},{8,0},{12,4},{16,24},{20,28},{24,16},{28,20},{32,40},... | collective-permute-start | bytes 56456 | tf_op jit(solution)/shard_map/ppermute | solution.py:22
  440.2 14.0 %collective-permute-done.66 = f32[16,588]{1,0:T(8,128)S(1)} collective-permute-done((f32[16,588]{1,0:T(8,128)S(1)}, f32[16,588]{1,0:T(8,128)S(1)}, u32[]{:S(2)}, u32[]{:S(2)}) %collective-permute-start.66) | collective-permute-done | bytes 37664 | tf_op jit(solution)/shard_map/ppermute | solution.py:22
  468.6 4.3 collective-permute-done.24
  472.9 5.6 %pad_maximum_fusion = (f32[10,35,24,128]{3,1,2,0:T(8,128)S(1)}, f32[10,35,24,128]{3,1,2,0:T(8,128)}) fusion(f32[10,3,24,128]{3,1,2,0:T(4,128)} %copy-done.10, f32[3,32,24,128]{3,1,2,0:T(8,128)} %copy-done.4, f32[4,32,24,128]{3,1,2,0:T(8,128)} %bitcast.171, f32[3,32,24,128]{3,1,2,0:T(8,128)} %collective-permute-done.21, ...), kind=kLoop, calls=%fused_computation | loop fusion | flops 6451200 | bytes 13271040 | tf_op jit(solution)/shard_map/concatenate | solution.py:16
  478.7 23.2 %fusion.173 = bf16[4,32,24,128]{3,1,2,0:T(8,128)(2,1)} fusion(f32[10,35,24,128]{3,1,2,0:T(8,128)} %get-tuple-element.70, f32[4,32,24,128]{3,1,2,0:T(8,128)} %bitcast.172, f32[3,32,24,128]{3,1,2,0:T(8,128)} %collective-permute-done.21, f32[10,35,24,128]{3,1,2,0:T(8,128)S(1)} %get-tuple-element.69, f32[3,32,24,128]{3,1,2,0:T(8,128)} %copy-done.4, ...), kind=kLoop, calls=%fused_computation.346 | loop fusion | flops 41287680 | bytes 72953856 | tf_op jit(solution)/shard_map/convert_element_type | solution.py:222
  (663 shorter events, 229.5 us)
Async XLA Ops:
  7.2 173.0 %all-gather.5.cloned.1.call-start = ((), (), s32[]{:S(2)}) async-start(), calls=%async_computation.2 | async-start | bytes 3932160 | tf_op jit(solution)/shard_map/all_gather | solution.py:157
  8.1 20.8 %collective-permute-start.12 = (bf16[48,512]{1,0:T(8,128)(2,1)S(1)}, bf16[48,512]{1,0:T(8,128)(2,1)}, u32[]{:S(2)}, u32[]{:S(2)}) collective-permute-start(bf16[48,512]{1,0:T(8,128)(2,1)S(1)} %get-tuple-element.132), channel_id=1, source_target_pairs={{0,64},{4,68},{8,72},{12,76},{16,80},{20,84},{24,88},{28,92},{32,9... | collective-permute-start | bytes 147464 | tf_op jit(solution)/shard_map/ppermute | solution.py:22
  11.4 20.6 %collective-permute-start.7 = (bf16[48,512]{1,0:T(8,128)(2,1)S(1)}, bf16[48,512]{1,0:T(8,128)(2,1)S(1)}, u32[]{:S(2)}, u32[]{:S(2)}) collective-permute-start(bf16[48,512]{1,0:T(8,128)(2,1)S(1)} %get-tuple-element.133), channel_id=1, source_target_pairs={{0,16},{4,20},{8,24},{12,28},{16,0},{20,4},{24,8},{28,12},{32,48},... | collective-permute-start | bytes 147464 | tf_op jit(solution)/shard_map/ppermute | solution.py:22
  15.3 55.2 %collective-permute-start.1 = (bf16[2,16,6144]{2,1,0:T(8,128)(2,1)}, bf16[2,16,6144]{2,1,0:T(8,128)(2,1)}, u32[]{:S(2)}, u32[]{:S(2)}) collective-permute-start(bf16[2,16,6144]{2,1,0:T(8,128)(2,1)} %get-tuple-element.81), channel_id=1, source_target_pairs={{0,1},{1,3},{2,0},{3,2},{4,5},{5,7},{6,4},{7,6},{8,9},{9,11},{10,8... | collective-permute-start | bytes 1179656 | tf_op jit(solution)/shard_map/ppermute | solution.py:107
  15.8 56.2 %collective-permute-start = (bf16[2,16,6144]{2,1,0:T(8,128)(2,1)}, bf16[2,16,6144]{2,1,0:T(8,128)(2,1)}, u32[]{:S(2)}, u32[]{:S(2)}) collective-permute-start(bf16[2,16,6144]{2,1,0:T(8,128)(2,1)} %get-tuple-element.82), channel_id=1, source_target_pairs={{0,0},{1,2},{2,1},{3,3},{4,4},{5,6},{6,5},{7,7},{8,8},{9,10},{10,9... | collective-permute-start | bytes 1179656 | tf_op jit(solution)/shard_map/ppermute | solution.py:106
  26.4 53.7 %collective-permute-start.18 = (bf16[3,32,24,128]{3,1,2,0:T(8,128)(2,1)}, bf16[3,32,24,128]{3,1,2,0:T(8,128)(2,1)S(1)}, u32[]{:S(2)}, u32[]{:S(2)}) collective-permute-start(bf16[3,32,24,128]{3,1,2,0:T(8,128)(2,1)} %bitcast.24), channel_id=1, source_target_pairs={{4,0},{8,4},{12,8},{16,12},{20,16},{24,20},{28,24},{32,28},{36,32}... | collective-permute-start | bytes 1769480 | tf_op jit(solution)/shard_map/ppermute | solution.py:15
  45.0 18.4 %collective-permute-start.4 = (bf16[192,512]{1,0:T(8,128)(2,1)S(1)}, bf16[192,512]{1,0:T(8,128)(2,1)S(1)}, u32[]{:S(2)}, u32[]{:S(2)}) collective-permute-start(bf16[192,512]{1,0:T(8,128)(2,1)S(1)} %fusion.197), channel_id=1, source_target_pairs={{0,32},{4,36},{8,40},{12,44},{16,48},{20,52},{24,56},{28,60},{32,0... | collective-permute-start | bytes 589832 | tf_op jit(solution)/shard_map/ppermute | solution.py:22
  48.8 18.0 %collective-permute-start.9 = (bf16[192,512]{1,0:T(8,128)(2,1)S(1)}, bf16[192,512]{1,0:T(8,128)(2,1)S(1)}, u32[]{:S(2)}, u32[]{:S(2)}) collective-permute-start(bf16[192,512]{1,0:T(8,128)(2,1)S(1)} %fusion.195), channel_id=1, source_target_pairs={{0,4},{4,0},{8,12},{12,8},{16,20},{20,16},{24,28},{28,24},{32,36},... | collective-permute-start | bytes 589832 | tf_op jit(solution)/shard_map/ppermute | solution.py:22
  63.4 18.4 %collective-permute-start.17 = (bf16[3,32,24,128]{3,1,2,0:T(8,128)(2,1)}, bf16[3,32,24,128]{3,1,2,0:T(8,128)(2,1)}, u32[]{:S(2)}, u32[]{:S(2)}) collective-permute-start(bf16[3,32,24,128]{3,1,2,0:T(8,128)(2,1)} %bitcast.22), channel_id=1, source_target_pairs={{0,4},{4,8},{8,12},{12,16},{16,20},{20,24},{24,28},{28,32},{32,36}... | collective-permute-start | bytes 1769480 | tf_op jit(solution)/shard_map/ppermute | solution.py:14
  66.8 31.0 %collective-permute-start.5 = (bf16[384,512]{1,0:T(8,128)(2,1)}, bf16[384,512]{1,0:T(8,128)(2,1)}, u32[]{:S(2)}, u32[]{:S(2)}) collective-permute-start(bf16[384,512]{1,0:T(8,128)(2,1)} %fusion.188), channel_id=1, source_target_pairs={{0,8},{4,12},{8,0},{12,4},{16,24},{20,28},{24,16},{28,20},{32,40},... | collective-permute-start | bytes 1179656 | tf_op jit(solution)/shard_map/ppermute | solution.py:22
  70.5 23.1 %collective-permute-start.10 = (bf16[384,512]{1,0:T(8,128)(2,1)}, bf16[384,512]{1,0:T(8,128)(2,1)}, u32[]{:S(2)}, u32[]{:S(2)}) collective-permute-start(bf16[384,512]{1,0:T(8,128)(2,1)} %fusion.186), channel_id=1, source_target_pairs={{0,32},{4,36},{8,40},{12,44},{16,48},{20,52},{24,56},{28,60},{32,0... | collective-permute-start | bytes 1179656 | tf_op jit(solution)/shard_map/ppermute | solution.py:22
  72.0 18.2 %collective-permute-start.15 = (bf16[384,512]{1,0:T(8,128)(2,1)}, bf16[384,512]{1,0:T(8,128)(2,1)}, u32[]{:S(2)}, u32[]{:S(2)}) collective-permute-start(bf16[384,512]{1,0:T(8,128)(2,1)} %fusion.184), channel_id=1, source_target_pairs={{0,4},{4,0},{8,12},{12,8},{16,20},{20,16},{24,28},{28,24},{32,36},... | collective-permute-start | bytes 1179656 | tf_op jit(solution)/shard_map/ppermute | solution.py:22
  83.0 18.8 %collective-permute-start.19 = (bf16[10,3,24,128]{3,1,2,0:T(4,128)(2,1)S(1)}, bf16[10,3,24,128]{3,1,2,0:T(4,128)(2,1)S(1)}, u32[]{:S(2)}, u32[]{:S(2)}) collective-permute-start(bf16[10,3,24,128]{3,1,2,0:T(4,128)(2,1)S(1)} %get-tuple-element.73), channel_id=1, source_target_pairs={{0,1},{1,2},{2,3},{4,5},{5,6},{6,7},{8,9},{9,10},{10,11},{12,13},{... | collective-permute-start | bytes 552968 | tf_op jit(solution)/shard_map/ppermute | solution.py:14
  84.9 16.9 %collective-permute-start.20 = (bf16[10,3,24,128]{3,1,2,0:T(4,128)(2,1)S(1)}, bf16[10,3,24,128]{3,1,2,0:T(4,128)(2,1)}, u32[]{:S(2)}, u32[]{:S(2)}) collective-permute-start(bf16[10,3,24,128]{3,1,2,0:T(4,128)(2,1)S(1)} %get-tuple-element.74), channel_id=1, source_target_pairs={{1,0},{2,1},{3,2},{5,4},{6,5},{7,6},{9,8},{10,9},{11,10},{13,12},{... | collective-permute-start | bytes 552968 | tf_op jit(solution)/shard_map/ppermute | solution.py:15
  92.9 17.7 %collective-permute-start.16 = (bf16[768,512]{1,0:T(8,128)(2,1)}, bf16[768,512]{1,0:T(8,128)(2,1)}, u32[]{:S(2)}, u32[]{:S(2)}) collective-permute-start(bf16[768,512]{1,0:T(8,128)(2,1)} %fusion.175), channel_id=1, source_target_pairs={{0,32},{4,36},{8,40},{12,44},{16,48},{20,52},{24,56},{28,60},{32,0... | collective-permute-start | bytes 2359304 | tf_op jit(solution)/shard_map/ppermute | solution.py:22
  96.2 17.4 %collective-permute-start.11 = (bf16[768,512]{1,0:T(8,128)(2,1)}, bf16[768,512]{1,0:T(8,128)(2,1)}, u32[]{:S(2)}, u32[]{:S(2)}) collective-permute-start(bf16[768,512]{1,0:T(8,128)(2,1)} %fusion.177), channel_id=1, source_target_pairs={{0,8},{4,12},{8,0},{12,4},{16,24},{20,28},{24,16},{28,20},{32,40},... | collective-permute-start | bytes 2359304 | tf_op jit(solution)/shard_map/ppermute | solution.py:22
  99.6 17.6 %collective-permute-start.6 = (bf16[768,512]{1,0:T(8,128)(2,1)S(1)}, bf16[768,512]{1,0:T(8,128)(2,1)S(1)}, u32[]{:S(2)}, u32[]{:S(2)}) collective-permute-start(bf16[768,512]{1,0:T(8,128)(2,1)S(1)} %fusion.179), channel_id=1, source_target_pairs={{0,4},{4,0},{8,12},{12,8},{16,20},{20,16},{24,28},{28,24},{32,36},... | collective-permute-start | bytes 2359304 | tf_op jit(solution)/shard_map/ppermute | solution.py:22
  146.2 67.6 %all-gather.3.cloned.1.call-start = ((), (), s32[]{:S(2)}) async-start(), calls=%async_computation.1 | async-start | bytes 3932160 | tf_op jit(solution)/shard_map/all_gather | solution.py:139
  146.9 166.3 %reduce-scatter.2.cloned.1.call-start = ((), (), s32[]{:S(2)}) async-start(), calls=%async_computation.3 | async-start | bytes 7864320 | tf_op jit(solution)/shard_map/reduce_scatter | solution.py:173
  246.4 16.4 %collective-permute-start.25 = (bf16[768,256]{1,0:T(8,128)(2,1)S(1)}, bf16[768,256]{1,0:T(8,128)(2,1)S(1)}, u32[]{:S(2)}, u32[]{:S(2)}) collective-permute-start(bf16[768,256]{1,0:T(8,128)(2,1)S(1)} %dynamic-slice_convert_fusion.5), channel_id=1, source_target_pairs={{0,4},{4,0},{8,12},{12,8},{16,20},{20,16},{24,28},{28,24},{32,36},... | collective-permute-start | bytes 1179656 | tf_op jit(solution)/shard_map/ppermute | solution.py:22
  253.2 18.1 %collective-permute-start.51 = (bf16[384,256]{1,0:T(8,128)(2,1)S(1)}, bf16[384,256]{1,0:T(8,128)(2,1)S(1)}, u32[]{:S(2)}, u32[]{:S(2)}) collective-permute-start(bf16[384,256]{1,0:T(8,128)(2,1)S(1)} %dynamic-slice_convert_fusion.6), channel_id=1, source_target_pairs={{0,4},{4,0},{8,12},{12,8},{16,20},{20,16},{24,28},{28,24},{32,36},... | collective-permute-start | bytes 589832 | tf_op jit(solution)/shard_map/ppermute | solution.py:22
  295.8 68.0 %collective-permute-start.38 = (f32[96,256]{1,0:T(8,128)S(1)}, f32[96,256]{1,0:T(8,128)}, u32[]{:S(2)}, u32[]{:S(2)}) collective-permute-start(f32[96,256]{1,0:T(8,128)S(1)} %constant_dynamic-slice_fusion.25), channel_id=1, source_target_pairs={{0,16},{4,20},{8,24},{12,28},{16,0},{20,4},{24,8},{28,12},{32,48},... | collective-permute-start | bytes 294920 | tf_op jit(solution)/shard_map/ppermute | solution.py:22
  297.3 77.4 %collective-permute-start.33 = (f32[96,256]{1,0:T(8,128)S(1)}, f32[96,256]{1,0:T(8,128)S(1)}, u32[]{:S(2)}, u32[]{:S(2)}) collective-permute-start(f32[96,256]{1,0:T(8,128)S(1)} %constant_dynamic-slice_fusion.28), channel_id=1, source_target_pairs={{0,64},{4,68},{8,72},{12,76},{16,80},{20,84},{24,88},{28,92},{32,9... | collective-permute-start | bytes 294920 | tf_op jit(solution)/shard_map/ppermute | solution.py:22
  301.1 86.0 %collective-permute-start.44 = (f32[48,256]{1,0:T(8,128)}, f32[48,256]{1,0:T(8,128)}, u32[]{:S(2)}, u32[]{:S(2)}) collective-permute-start(f32[48,256]{1,0:T(8,128)} %constant_dynamic-slice_fusion.21), channel_id=1, source_target_pairs={{0,64},{4,68},{8,72},{12,76},{16,80},{20,84},{24,88},{28,92},{32,9... | collective-permute-start | bytes 147464 | tf_op jit(solution)/shard_map/ppermute | solution.py:22
  302.2 93.1 %collective-permute-start.54 = (f32[48,256]{1,0:T(8,128)}, f32[48,256]{1,0:T(8,128)}, u32[]{:S(2)}, u32[]{:S(2)}) collective-permute-start(f32[48,256]{1,0:T(8,128)} %constant_dynamic-slice_fusion.15), channel_id=1, source_target_pairs={{0,64},{4,68},{8,72},{12,76},{16,80},{20,84},{24,88},{28,92},{32,9... | collective-permute-start | bytes 147464 | tf_op jit(solution)/shard_map/ppermute | solution.py:22
  305.9 131.8 %collective-permute-start.49 = (f32[48,256]{1,0:T(8,128)}, f32[48,256]{1,0:T(8,128)}, u32[]{:S(2)}, u32[]{:S(2)}) collective-permute-start(f32[48,256]{1,0:T(8,128)} %constant_dynamic-slice_fusion.18), channel_id=1, source_target_pairs={{0,16},{4,20},{8,24},{12,28},{16,0},{20,4},{24,8},{28,12},{32,48},... | collective-permute-start | bytes 147464 | tf_op jit(solution)/shard_map/ppermute | solution.py:22
  371.4 40.0 %collective-permute-start.29 = (f32[48,256]{1,0:T(8,128)}, f32[48,256]{1,0:T(8,128)}, u32[]{:S(2)}, u32[]{:S(2)}) collective-permute-start(f32[48,256]{1,0:T(8,128)} %constant_dynamic-slice_fusion.30), channel_id=1, source_target_pairs={{0,64},{4,68},{8,72},{12,76},{16,80},{20,84},{24,88},{28,92},{32,9... | collective-permute-start | bytes 147464 | tf_op jit(solution)/shard_map/ppermute | solution.py:22
  386.4 30.3 %collective-permute-start.39 = (f32[48,256]{1,0:T(8,128)S(1)}, f32[48,256]{1,0:T(8,128)S(1)}, u32[]{:S(2)}, u32[]{:S(2)}) collective-permute-start(f32[48,256]{1,0:T(8,128)S(1)} %constant_dynamic-slice_fusion.24), channel_id=1, source_target_pairs={{0,64},{4,68},{8,72},{12,76},{16,80},{20,84},{24,88},{28,92},{32,9... | collective-permute-start | bytes 147464 | tf_op jit(solution)/shard_map/ppermute | solution.py:22
  402.5 53.2 %collective-permute-start.22 = (f32[3,32,24,128]{3,1,2,0:T(8,128)}, f32[3,32,24,128]{3,1,2,0:T(8,128)S(1)}, u32[]{:S(2)}, u32[]{:S(2)}) collective-permute-start(f32[3,32,24,128]{3,1,2,0:T(8,128)} %bitcast.80), channel_id=1, source_target_pairs={{4,0},{8,4},{12,8},{16,12},{20,16},{24,20},{28,24},{32,28},{36,32}... | collective-permute-start | bytes 3538952 | tf_op jit(solution)/shard_map/ppermute | solution.py:15
  404.4 51.3 %collective-permute-start.21 = (f32[3,32,24,128]{3,1,2,0:T(8,128)}, f32[3,32,24,128]{3,1,2,0:T(8,128)}, u32[]{:S(2)}, u32[]{:S(2)}) collective-permute-start(f32[3,32,24,128]{3,1,2,0:T(8,128)} %bitcast.78), channel_id=1, source_target_pairs={{0,4},{4,8},{8,12},{12,16},{16,20},{20,24},{24,28},{28,32},{32,36}... | collective-permute-start | bytes 3538952 | tf_op jit(solution)/shard_map/ppermute | solution.py:14
  416.6 22.9 %collective-permute-start.34 = (f32[48,256]{1,0:T(8,128)S(1)}, f32[48,256]{1,0:T(8,128)S(1)}, u32[]{:S(2)}, u32[]{:S(2)}) collective-permute-start(f32[48,256]{1,0:T(8,128)S(1)} %constant_dynamic-slice_fusion.27), channel_id=1, source_target_pairs={{0,16},{4,20},{8,24},{12,28},{16,0},{20,4},{24,8},{28,12},{32,48},... | collective-permute-start | bytes 147464 | tf_op jit(solution)/shard_map/ppermute | solution.py:22
  420.5 19.0 %collective-permute-start.65 = (f32[8,588]{1,0:T(8,128)S(1)}, f32[8,588]{1,0:T(8,128)S(1)}, u32[]{:S(2)}, u32[]{:S(2)}) collective-permute-start(f32[8,588]{1,0:T(8,128)S(1)} %fusion.213), channel_id=1, source_target_pairs={{0,8},{4,12},{8,0},{12,4},{16,24},{20,28},{24,16},{28,20},{32,40},... | collective-permute-start | bytes 56456 | tf_op jit(solution)/shard_map/ppermute | solution.py:22
  (147 other events, 1750.4 us)
Sparse Core Ops, SparseCore 0:
  146.3 33.8 all-gather.4
  181.8 31.8 all-gather.2
  226.5 86.7 reduce-scatter.1
